TPU v7x, 256 devices: a whole 4x4x8 slice. The times are simulated.
256 devices in a mesh: seq: 64 (over y, z, core), head: 4 (over x).
Axes of the slice: x: 4, y: 4, z: 8, core: 2. Of those that a mesh axis runs over, the one named last changes fastest.
Arguments:
- queries: bfloat16 [8192, 1024], P('seq', 'head'), may hold values from -6 to 6
- raw_keys: bfloat16 [8192, 1024], P('seq', 'head'), may hold values from -6 to 6
- values: bfloat16 [8192, 1024], P('seq', 'head'), may hold values from -6 to 6
- write_rate: float32 [8192, 8], P('seq', 'head'), may hold values from 0.0005 to 1
- out_weight: bfloat16 [1024, 1024], P('head'), may hold values from -0.1875 to 0.1875
- out_grad: bfloat16 [8192, 1024], P('seq', 'head'), may hold values from -6 to 6
Outputs:
- layer_out: bfloat16 [8192, 1024], P('seq', 'head')
- query_grad: bfloat16 [8192, 1024], P('seq', 'head')
- key_grad: bfloat16 [8192, 1024], P('seq', 'head')
- value_grad: bfloat16 [8192, 1024], P('seq', 'head')
- rate_grad: float32 [8192, 8], P('seq', 'head')
All inputs are finite; a program needn't handle non-finite values.
Results may differ from a plain program's by a relative error of at most 0.0049.
Values may be sent and summed in bfloat16 or wider, within the bound.
No kernel may reach another device: no remote copies, remote signals or barrier semaphores. Data moves between devices by JAX's collectives and lax.ppermute only.
A program may use at most 128 MiB of HBM per device.

v0:
```python
import jax
import jax.numpy as jnp
from jax import lax
from jax.sharding import PartitionSpec as P

BLOCK = 64
epsilon = 1e-06
highest = lax.Precision.HIGHEST


def prefix(part, axis, combine, identity, reverse):
    count = lax.axis_size(axis)
    place = lax.axis_index(axis)
    ahead = count - 1 - place if reverse else place
    gathered = jax.tree.map(lambda a: lax.all_gather(a, axis), part)
    state = jax.tree.map(lambda a, e: jnp.zeros_like(a) + jnp.asarray(e, a.dtype), part, identity)

    def one(turn, state):
        source = count - 1 - turn if reverse else turn
        return combine(
            state, jax.tree.map(lambda a: lax.dynamic_index_in_dim(a, source, 0, False), gathered)
        )

    return lax.fori_loop(0, ahead, one, state)


def unit_rows(array):
    return array * lax.rsqrt(jnp.sum(array * array, -1, keepdims=True) + epsilon)


def to_blocks(array, head_count):
    rows = array.shape[0]
    head_width = array.shape[1] // head_count
    return array.reshape(rows // BLOCK, BLOCK, head_count, head_width).transpose(2, 0, 1, 3)


def rate_blocks(decay_rate):
    rows = decay_rate.shape[0]
    head_count = decay_rate.shape[1]
    return decay_rate.reshape(rows // BLOCK, BLOCK, head_count).transpose(2, 0, 1)


def from_blocks(block_outputs):
    block_count, head_count, size, head_width = block_outputs.shape
    return block_outputs.transpose(0, 2, 1, 3).reshape(block_count * size, head_count * head_width)


def block_factors(query_blocks, key_blocks, value_blocks, rate_parts):
    unit_query = unit_rows(query_blocks)
    unit_key = unit_rows(key_blocks)
    size = unit_key.shape[-2]
    identity_block = jnp.eye(size, dtype=jnp.float32)
    key_gram = jnp.einsum(
        "hncd,hnsd->hncs", unit_key * rate_parts[..., None], unit_key, precision=highest
    )
    strict_lower = jnp.tril(key_gram, -1)
    result = identity_block - strict_lower
    power_term = strict_lower
    span_done = 2
    while span_done < size:
        power_term = jnp.einsum("hnij,hnjk->hnik", power_term, power_term, precision=highest)
        result = result + jnp.einsum("hnij,hnjk->hnik", result, power_term, precision=highest)
        span_done = span_done * 2
    scaled = result * rate_parts[..., None, :]
    key_mix = jnp.einsum("hncs,hnsd->hncd", scaled, unit_key, precision=highest)
    value_mix = jnp.einsum("hncs,hnsd->hncd", scaled, value_blocks, precision=highest)
    causal_scores = jnp.tril(jnp.einsum("hncd,hnsd->hncs", unit_query, unit_key, precision=highest))
    return (unit_query, unit_key, key_mix, value_mix, causal_scores)


def run_blocks(factors, start_state):
    moved = tuple((jnp.moveaxis(member, 1, 0) for member in factors))

    def advance_block(state, pieces):
        unit_query, unit_key, key_mix, value_mix, causal_scores = pieces
        innovation = value_mix - jnp.einsum("hcd,hde->hce", key_mix, state, precision=highest)
        block_out = jnp.einsum("hcd,hde->hce", unit_query, state, precision=highest)
        block_out = block_out + jnp.einsum(
            "hcs,hse->hce", causal_scores, innovation, precision=highest
        )
        state = state + jnp.einsum("hcd,hce->hde", unit_key, innovation, precision=highest)
        return (state, block_out)

    return lax.scan(advance_block, start_state, moved)


def compose(earlier, later):
    early_map, early_shift = earlier
    late_map, late_shift = later
    joined_map = jnp.einsum("hij,hjk->hik", late_map, early_map, precision=highest)
    joined_shift = jnp.einsum("hij,hjk->hik", late_map, early_shift, precision=highest) + late_shift
    return (joined_map, joined_shift)


def body(queries, raw_keys, values, write_rate, out_weight, out_grad):
    head_count = write_rate.shape[1]
    head_width = queries.shape[1] // head_count
    token_count = queries.shape[0]

    def factor_inputs(float_query, float_key, float_value, rates):
        return block_factors(
            to_blocks(float_query, head_count),
            to_blocks(float_key, head_count),
            to_blocks(float_value, head_count),
            rate_blocks(rates),
        )

    factors, pull_factors = jax.vjp(
        factor_inputs,
        queries.astype(jnp.float32),
        raw_keys.astype(jnp.float32),
        values.astype(jnp.float32),
        write_rate,
    )
    unit_query, unit_key, key_mix, value_mix, causal_scores = factors
    identity_heads = jnp.broadcast_to(
        jnp.eye(head_width, dtype=jnp.float32), (head_count, head_width, head_width)
    )
    zero_heads = jnp.zeros((head_count, head_width, head_width), jnp.float32)
    widened = (
        unit_query,
        unit_key,
        key_mix,
        jnp.concatenate([jnp.zeros_like(value_mix), value_mix], -1),
        causal_scores,
    )
    joined_state, joined_outputs = run_blocks(
        widened, jnp.concatenate([identity_heads, zero_heads], -1)
    )
    transition = joined_state[..., :head_width]
    offset = joined_state[..., head_width:]
    query_effect = joined_outputs[..., :head_width]
    attended_grad = lax.dot_general(
        lax.all_gather(out_grad, "head", axis=1, tiled=True),
        out_weight,
        (((1,), (1,)), ((), ())),
        preferred_element_type=jnp.float32,
    )
    grad_blocks = attended_grad.reshape(
        token_count // BLOCK, BLOCK, head_count, head_width
    ).transpose(0, 2, 1, 3)
    local_adjoint = jnp.einsum("nhcd,nhce->hde", query_effect, grad_blocks, precision=highest)
    unused_map, entry_state = prefix(
        (transition, offset), "seq", compose, (identity_heads, zero_heads), False
    )
    unused_adjoint_map, exit_adjoint = prefix(
        (jnp.swapaxes(transition, 1, 2), local_adjoint),
        "seq",
        compose,
        (identity_heads, zero_heads),
        True,
    )

    def run_from_entry(factor_tuple):
        return run_blocks(factor_tuple, entry_state)

    (final_state, block_outputs), pull_run = jax.vjp(run_from_entry, factors)
    factor_grads = pull_run((exit_adjoint, grad_blocks))
    query_part, key_part, value_part, rate_grad = pull_factors(factor_grads[0])
    attended_bf = from_blocks(block_outputs).astype(jnp.bfloat16)
    partial_out = jnp.dot(attended_bf, out_weight, preferred_element_type=jnp.float32)
    layer_out = lax.psum_scatter(partial_out, "head", scatter_dimension=1, tiled=True).astype(
        jnp.bfloat16
    )
    return (
        layer_out,
        query_part.astype(jnp.bfloat16),
        key_part.astype(jnp.bfloat16),
        value_part.astype(jnp.bfloat16),
        rate_grad,
    )


def solution(mesh):
    placed = (
        P("seq", "head"),
        P("seq", "head"),
        P("seq", "head"),
        P("seq", "head"),
        P("head", None),
        P("seq", "head"),
    )
    return jax.shard_map(
        body,
        mesh=mesh,
        in_specs=placed,
        out_specs=(
            P("seq", "head"),
            P("seq", "head"),
            P("seq", "head"),
            P("seq", "head"),
            P("seq", "head"),
        ),
        check_vma=False,
    )
```

profile of v0, /device:TPU:8, one launch (start us, length us, event | category | flops | bytes accessed | tf_op | source)
XLA Modules:
  0.0 506.4 jit_solution(13383869806528043871)
XLA Ops:
  16.5 4.0 while.78
  20.5 12.6 %all_gather.33 = bf16[128,1024]{1,0:T(8,128)(2,1)S(1)} all-gather(bf16[128,256]{1,0:T(8,128)(2,1)S(1)} %copy-done.15), channel_id=1, replica_groups=mesh['seq'=64,'head'=4] {'head'}, dimensions={1}, use_global_device_ids=true | all-gather | bytes 327680 | tf_op jit(solution)/shard_map/all_gather | solution.py:134
  33.5 1.9 convolution_bitcast_fusion.4
  39.1 80.6 %all-gather.15.cloned.1.call-done = f32[128,128,128]{2,1,0:T(8,128)} async-done(((f32[2,128,128]{2,1,0:T(8,128)}), f32[128,128,128]{2,1,0:T(8,128)}) %all-gather.15.cloned.1.call-update) | async-done | bytes 8388624 | tf_op jit(solution)/shard_map/all_gather | solution.py:15
  119.6 82.6 %all-gather.13.cloned.1.call-done = f32[128,128,128]{2,1,0:T(8,128)} async-done(((f32[2,128,128]{2,1,0:T(8,128)}), f32[128,128,128]{2,1,0:T(8,128)}) %all-gather.13.cloned.1.call-update) | async-done | bytes 8388624 | tf_op jit(solution)/shard_map/all_gather | solution.py:15
  202.2 60.8 %while.81 = (s32[]{:T(128)}, f32[2,128,128]{2,1,0:T(8,128)S(1)}, s32[]{:T(128)}, f32[64,2,128,128]{3,2,1,0:T(8,128)}, f32[64,2,128,128]{3,2,1,0:T(8,128)}, /*index=5*/s32[]{:T(128)}, s32[]{:T(128)}, s32[]{:T(128)}, s32[]{:T(128)}) while((s32[]{:T(128)}, f32[2,128,128]{2,1,0:T(8,128)S(1)}, s32[]{:T(128)}, f32[64,2,128,128]{3,2,1,0:T(8,128)}, ...), condition=%wide.region_10.11_spmd, body=%wide.region_9.10_spmd.sunk | while | flops 50364420 | bytes 787595 | solution.py:24
  202.3 1.2 convolution_add_fusion.38
  203.6 1.2 convolution_add_fusion.38
  204.9 1.2 convolution_add_fusion.38
  206.2 1.2 convolution_add_fusion.38
  208.7 1.2 convolution_add_fusion.38
  211.3 1.2 convolution_add_fusion.38
  212.6 1.2 convolution_add_fusion.38
  213.9 1.2 convolution_add_fusion.38
  215.2 1.3 convolution_add_fusion.38
  217.8 1.2 convolution_add_fusion.38
  219.1 1.2 convolution_add_fusion.38
  220.4 1.2 convolution_add_fusion.38
  221.7 1.2 convolution_add_fusion.38
  223.0 1.2 convolution_add_fusion.38
  224.3 1.2 convolution_add_fusion.38
  225.6 1.2 convolution_add_fusion.38
  228.1 1.2 convolution_add_fusion.38
  229.4 1.2 convolution_add_fusion.38
  230.7 1.2 convolution_add_fusion.38
  233.3 1.2 convolution_add_fusion.38
  235.9 1.2 convolution_add_fusion.38
  237.2 1.2 convolution_add_fusion.38
  238.5 1.2 convolution_add_fusion.38
  239.8 1.2 convolution_add_fusion.38
  241.1 1.2 convolution_add_fusion.38
  242.4 1.2 convolution_add_fusion.38
  244.9 1.2 convolution_add_fusion.38
  246.2 1.2 convolution_add_fusion.38
  251.4 1.2 convolution_add_fusion.38
  252.7 1.2 convolution_add_fusion.38
  255.3 1.2 convolution_add_fusion.38
  256.6 1.2 convolution_add_fusion.38
  257.9 1.3 convolution_add_fusion.38
  259.2 1.3 convolution_add_fusion.38
  261.8 1.2 convolution_add_fusion.38
  263.1 21.8 %all-gather.9.cloned.1.call-done = f32[128,128,128]{2,1,0:T(8,128)} async-done(((f32[2,128,128]{2,1,0:T(8,128)}), f32[128,128,128]{2,1,0:T(8,128)}) %all-gather.9.cloned.1.call-update) | async-done | bytes 8388624 | tf_op jit(solution)/shard_map/all_gather | solution.py:15
  284.9 82.4 %all-gather.11.cloned.1.call-done = f32[128,128,128]{2,1,0:T(8,128)} async-done(((f32[2,128,128]{2,1,0:T(8,128)}), f32[128,128,128]{2,1,0:T(8,128)}) %all-gather.11.cloned.1.call-update) | async-done | bytes 8388624 | tf_op jit(solution)/shard_map/all_gather | solution.py:15
  367.3 20.8 %while.79 = (s32[]{:T(128)}, f32[2,128,128]{2,1,0:T(8,128)S(1)}, s32[]{:T(128)}, f32[64,2,128,128]{3,2,1,0:T(8,128)}, f32[64,2,128,128]{3,2,1,0:T(8,128)}, /*index=5*/s32[]{:T(128)}, s32[]{:T(128)}, s32[]{:T(128)}) while((s32[]{:T(128)}, f32[2,128,128]{2,1,0:T(8,128)S(1)}, s32[]{:T(128)}, f32[64,2,128,128]{3,2,1,0:T(8,128)}, ...), condition=%wide.region_5.6_spmd, body=%wide.region_4.5_spmd.sunk | while | flops 50364420 | bytes 787575 | solution.py:24
  388.2 3.5 while.80
  394.3 10.4 %while.82 = (s32[]{:T(128)}, f32[2,128,128]{2,1,0:T(8,128)S(1)}, f32[2,2,64,128]{3,2,0,1:T(8,128)}, f32[2,2,64,128]{3,2,0,1:T(8,128)}, f32[2,2,64,128]{3,2,1,0:T...) while((s32[]{:T(128)}, f32[2,128,128]{2,1,0:T(8,128)S(1)}, ...), condition=%wide.region_12.13_spmd, body=%wide.region_11.12_spmd.sunk | while | flops 176275456 | bytes 2367137 | solution.py:84
  420.9 77.4 %reduce-scatter.2.cloned.1.call-done = f32[128,256]{1,0:T(8,128)} async-done(((f32[128,1024]{1,0:T(8,128)}), f32[128,256]{1,0:T(8,128)}) %reduce-scatter.2.cloned.1.call-update) | async-done | bytes 131088 | tf_op jit(solution)/shard_map/reduce_scatter | solution.py:162
  498.3 1.5 convert_element_type.51
  (274 shorter events, 84.4 us)
Async XLA Ops:
  7.2 25.9 %copy-start = (bf16[256,1024]{1,0:T(8,128)(2,1)S(1)}, bf16[256,1024]{1,0:T(8,128)(2,1)}, u32[]{:S(2)}) copy-start(bf16[256,1024]{1,0:T(8,128)(2,1)} %param.20) | copy-start | bytes 1572868
  7.2 112.4 %all-gather.15.cloned.1.call-start = ((), (), s32[]{:S(2)}) async-start(), calls=%async_computation.5 | async-start | bytes 8519680 | tf_op jit(solution)/shard_map/all_gather | solution.py:15
  7.2 4.0 copy-start.10
  8.4 3.7 copy-start.20
  9.4 2.7 copy-start.18
  10.3 0.8 copy-start.13
  10.3 4.7 copy-start.16
  11.6 1.4 copy-start.3
  12.4 8.1 %copy-start.15 = (bf16[128,256]{1,0:T(8,128)(2,1)S(1)}, bf16[128,256]{1,0:T(8,128)(2,1)}, u32[]{:S(2)}) copy-start(bf16[128,256]{1,0:T(8,128)(2,1)} %param.21) | copy-start | bytes 196612
  12.7 3.8 copy-start.1
  14.7 0.6 copy-start.9
  35.4 166.8 %all-gather.13.cloned.1.call-start = ((), (), s32[]{:S(2)}) async-start(), calls=%async_computation.4 | async-start | bytes 8519680 | tf_op jit(solution)/shard_map/all_gather | solution.py:15
  37.0 247.8 %all-gather.9.cloned.1.call-start = ((), (), s32[]{:S(2)}) async-start(), calls=%async_computation.2 | async-start | bytes 8519680 | tf_op jit(solution)/shard_map/all_gather | solution.py:15
  37.8 329.5 %all-gather.11.cloned.1.call-start = ((), (), s32[]{:S(2)}) async-start(), calls=%async_computation.3 | async-start | bytes 8519680 | tf_op jit(solution)/shard_map/all_gather | solution.py:15
  38.3 460.0 %reduce-scatter.2.cloned.1.call-start = ((), (), s32[]{:S(2)}) async-start(), calls=%async_computation.1 | async-start | bytes 655360 | tf_op jit(solution)/shard_map/reduce_scatter | solution.py:162
  392.4 17.0 %copy-start.2 = (f32[2,2,64,64]{3,2,1,0:T(8,128)S(1)}, f32[2,2,64,64]{3,2,1,0:T(8,128)}, u32[]{:S(2)}) copy-start(f32[2,2,64,64]{3,2,1,0:T(8,128)} %copy-done.1) | copy-start | bytes 196612
  394.3 17.3 %copy-start.4 = (f32[2,2,64,64]{3,2,1,0:T(8,128)S(1)}, f32[2,2,64,64]{3,2,1,0:T(8,128)}, u32[]{:S(2)}) copy-start(f32[2,2,64,64]{3,2,1,0:T(8,128)} %copy-done.3) | copy-start | bytes 196612
  404.7 8.1 %copy-start.11 = (f32[64,64]{1,0:T(8,128)S(1)}, f32[64,64]{1,0:T(8,128)}, u32[]{:S(2)}) copy-start(f32[64,64]{1,0:T(8,128)} %copy-done.10) | copy-start | bytes 49156
  404.7 9.2 %copy-start.14 = (pred[64,64]{1,0:T(8,128)(4,1)S(1)}, pred[64,64]{1,0:T(8,128)(4,1)}, u32[]{:S(2)}) copy-start(pred[64,64]{1,0:T(8,128)(4,1)} %copy-done.13) | copy-start | bytes 12292
  404.7 10.0 %copy-start.7 = (f32[2,2,64,64]{3,2,1,0:T(8,128)S(1)}, f32[2,2,64,64]{3,2,1,0:T(8,128)}, u32[]{:S(2)}) copy-start(f32[2,2,64,64]{3,2,1,0:T(8,128)} %get-tuple-element.516) | copy-start | bytes 196612
  404.7 10.0 %copy-start.17 = (f32[2,2,64]{2,1,0:T(2,128)S(1)}, f32[2,2,64]{2,1,0:T(2,128)}, u32[]{:S(2)}) copy-start(f32[2,2,64]{2,1,0:T(2,128)} %copy-done.16) | copy-start | bytes 3076
  404.7 10.5 %copy-start.6 = (f32[2,2,64,128]{3,2,0,1:T(8,128)S(1)}, f32[2,2,64,128]{3,2,0,1:T(8,128)}, u32[]{:S(2)}) copy-start(f32[2,2,64,128]{3,2,0,1:T(8,128)} %get-tuple-element.517) | copy-start | bytes 393220
  404.8 11.0 %copy-start.21 = (f32[2,2,64]{2,1,0:T(2,128)S(1)}, f32[2,2,64]{2,1,0:T(2,128)}, u32[]{:S(2)}) copy-start(f32[2,2,64]{2,1,0:T(2,128)} %copy-done.20) | copy-start | bytes 3076
  404.8 11.0 %copy-start.12 = (bf16[2,2,64,128]{3,2,1,0:T(8,128)(2,1)S(1)}, bf16[2,2,64,128]{3,2,1,0:T(8,128)(2,1)}, u32[]{:S(2)}) copy-start(bf16[2,2,64,128]{3,2,1,0:T(8,128)(2,1)} %get-tuple-element.510) | copy-start | bytes 196612
  404.8 13.7 %copy-start.8 = (f32[2,2,64,128]{3,2,1,0:T(8,128)S(1)}, f32[2,2,64,128]{3,2,1,0:T(8,128)}, u32[]{:S(2)}) copy-start(f32[2,2,64,128]{3,2,1,0:T(8,128)} %get-tuple-element.519) | copy-start | bytes 393220
  404.8 14.8 %copy-start.5 = (f32[2,2,64,128]{3,2,0,1:T(8,128)S(1)}, f32[2,2,64,128]{3,2,0,1:T(8,128)}, u32[]{:S(2)}) copy-start(f32[2,2,64,128]{3,2,0,1:T(8,128)} %get-tuple-element.515) | copy-start | bytes 393220
  404.8 15.3 %copy-start.19 = (f32[2,2,64]{2,1,0:T(2,128)S(1)}, f32[2,2,64]{2,1,0:T(2,128)}, u32[]{:S(2)}) copy-start(f32[2,2,64]{2,1,0:T(2,128)} %copy-done.18) | copy-start | bytes 3076
Sparse Core Ops, SparseCore 0:
  35.6 84.0 all-gather.14
  122.4 79.7 all-gather.12
  205.0 79.8 all-gather.8
  287.5 79.7 all-gather.10
  417.1 81.1 reduce-scatter.1
where the time goes:
time: 508 us; the launch traced here: 506 us
  waiting for transfers between devices  346 us (68%)
  matrix products  115 us (23%)
  between operations  14.6 us (3%)
  blocking collectives  12.6 us (2%)
  local copies, waits for them, and re-layouts  12 us (2%)
    all_gather x4, waiting for transfers between devices, prefix(): gathered = jax.tree.map(lambda a: lax.all_gather(a, axis), part)  267 us
    dot_general x63, matrix products, compose(): jnp.einsum('hij,hjk->hik', late_map, early_shift, precision=highest)  78.3 us
    reduce_scatter x1, waiting for transfers between devices, body(): lax.psum_scatter(partial_out, 'head', scatter_dimension=1, tiled=True)  77.4 us
    all_gather x1, blocking collectives, body(): lax.all_gather(out_grad, 'head', axis=1, tiled=True)  12.6 us
  transfers between devices with their start and end apart: 5, of which 5 were waited for; matrix products, arithmetic and copies ran while one was open for 13% of the time, Pallas kernels for 0%

commit v1 on v0

--- a/solution.py
+++ b/solution.py
@@ -131,7 +131,9 @@
     offset = joined_state[..., head_width:]
     query_effect = joined_outputs[..., :head_width]
     attended_grad = lax.dot_general(
-        lax.all_gather(out_grad, "head", axis=1, tiled=True),
+        jnp.concatenate(
+            lax.all_to_all(jnp.stack([out_grad] * lax.axis_size("head")), "head", 0, 0), axis=1
+        ),
         out_weight,
         (((1,), (1,)), ((), ())),
         preferred_element_type=jnp.float32,

time: 508 us -> 475 us (0.935)
  the two profiles are of different devices: /device:TPU:8 before, /device:TPU:2 now
where the time goes in v1:
time: 475 us; the launch traced here: 474 us
  waiting for transfers between devices  313 us (66%)
  matrix products  114 us (24%)
  between operations  14.5 us (3%)
  local copies, waits for them, and re-layouts  14.4 us (3%)
  blocking collectives  9.85 us (2%)
    all_gather x4, waiting for transfers between devices, prefix(): gathered = jax.tree.map(lambda a: lax.all_gather(a, axis), part)  313 us
    dot_general x63, matrix products, compose(): jnp.einsum('hij,hjk->hik', late_map, early_shift, precision=highest)  78.2 us
    all_to_all x1, blocking collectives, body(): lax.all_to_all(jnp.stack([out_grad] * lax.axis_size('head')), 'head', 0, 0)  9.85 us
  transfers between devices with their start and end apart: 5, of which 4 were waited for; matrix products, arithmetic and copies ran while one was open for 25% of the time, Pallas kernels for 0%

profile of v1, /device:TPU:2, one launch (start us, length us, event | category | flops | bytes accessed | tf_op | source)
XLA Modules:
  0.0 473.6 jit_solution(9930602397456704419)
XLA Ops:
  16.8 3.9 while.78
  24.0 9.9 %all_to_all.5 = bf16[4,128,256]{2,1,0:T(8,128)(2,1)S(1)} all-to-all(bf16[4,128,256]{2,1,0:T(8,128)(2,1)S(1)} %stack.2), channel_id=1, replica_groups=mesh['seq'=64,'head'=4] {'head'}, dimensions={0} | all-to-all | bytes 524288 | tf_op jit(solution)/shard_map/all_to_all | solution.py:135
  34.6 1.9 convolution_bitcast_fusion.5
  37.2 70.4 %all-gather.9.cloned.1.call-done = f32[128,128,128]{2,1,0:T(8,128)} async-done(((f32[2,128,128]{2,1,0:T(8,128)}), f32[128,128,128]{2,1,0:T(8,128)}) %all-gather.9.cloned.1.call-update) | async-done | bytes 8388624 | tf_op jit(solution)/shard_map/all_gather | solution.py:15
  107.6 82.6 %all-gather.11.cloned.1.call-done = f32[128,128,128]{2,1,0:T(8,128)} async-done(((f32[2,128,128]{2,1,0:T(8,128)}), f32[128,128,128]{2,1,0:T(8,128)}) %all-gather.11.cloned.1.call-update) | async-done | bytes 8388624 | tf_op jit(solution)/shard_map/all_gather | solution.py:15
  190.3 3.5 while.80
  195.7 77.2 %all-gather.13.cloned.1.call-done = f32[128,128,128]{2,1,0:T(8,128)} async-done(((f32[2,128,128]{2,1,0:T(8,128)}), f32[128,128,128]{2,1,0:T(8,128)}) %all-gather.13.cloned.1.call-update) | async-done | bytes 8388624 | tf_op jit(solution)/shard_map/all_gather | solution.py:15
  273.0 82.4 %all-gather.15.cloned.1.call-done = f32[128,128,128]{2,1,0:T(8,128)} async-done(((f32[2,128,128]{2,1,0:T(8,128)}), f32[128,128,128]{2,1,0:T(8,128)}) %all-gather.15.cloned.1.call-update) | async-done | bytes 8388624 | tf_op jit(solution)/shard_map/all_gather | solution.py:15
  355.3 81.6 %while.81 = (s32[]{:T(128)}, f32[2,128,128]{2,1,0:T(8,128)S(1)}, s32[]{:T(128)}, f32[64,2,128,128]{3,2,1,0:T(8,128)}, f32[64,2,128,128]{3,2,1,0:T(8,128)}, /*index=5*/s32[]{:T(128)}, s32[]{:T(128)}, s32[]{:T(128)}, s32[]{:T(128)}) while((s32[]{:T(128)}, f32[2,128,128]{2,1,0:T(8,128)S(1)}, s32[]{:T(128)}, f32[64,2,128,128]{3,2,1,0:T(8,128)}, ...), condition=%wide.region_10.11_spmd, body=%wide.region_9.10_spmd.sunk | while | flops 50364420 | bytes 787595 | solution.py:24
  355.4 1.2 convolution_add_fusion.38
  356.7 1.2 convolution_add_fusion.38
  358.0 1.2 convolution_add_fusion.38
  359.3 1.2 convolution_add_fusion.38
  360.6 1.2 convolution_add_fusion.38
  361.8 1.2 convolution_add_fusion.38
  363.1 1.2 convolution_add_fusion.38
  364.4 1.2 convolution_add_fusion.38
  365.7 1.2 convolution_add_fusion.38
  367.0 1.2 convolution_add_fusion.38
  368.3 1.2 convolution_add_fusion.38
  369.6 1.2 convolution_add_fusion.38
  370.9 1.2 convolution_add_fusion.38
  372.2 1.2 convolution_add_fusion.38
  373.5 1.2 convolution_add_fusion.38
  374.8 1.2 convolution_add_fusion.38
  376.1 1.2 convolution_add_fusion.38
  377.4 1.2 convolution_add_fusion.38
  378.7 1.2 convolution_add_fusion.38
  379.9 1.2 convolution_add_fusion.38
  381.2 1.2 convolution_add_fusion.38
  382.5 1.2 convolution_add_fusion.38
  383.8 1.2 convolution_add_fusion.38
  385.1 1.2 convolution_add_fusion.38
  386.4 1.2 convolution_add_fusion.38
  390.3 1.2 convolution_add_fusion.38
  394.1 1.2 convolution_add_fusion.38
  398.0 1.2 convolution_add_fusion.38
  401.9 1.2 convolution_add_fusion.38
  405.8 1.2 convolution_add_fusion.38
  409.6 1.2 convolution_add_fusion.38
  413.5 1.2 convolution_add_fusion.38
  417.4 1.2 convolution_add_fusion.38
  421.3 1.2 convolution_add_fusion.38
  425.1 1.2 convolution_add_fusion.38
  429.0 1.2 convolution_add_fusion.38
  432.9 1.2 convolution_add_fusion.38
  439.6 10.3 %while.82 = (s32[]{:T(128)}, f32[2,128,128]{2,1,0:T(8,128)S(1)}, f32[2,2,64,128]{3,2,0,1:T(8,128)}, f32[2,2,64,128]{3,2,0,1:T(8,128)}, f32[2,2,64,128]{3,2,1,0:T...) while((s32[]{:T(128)}, f32[2,128,128]{2,1,0:T(8,128)S(1)}, ...), condition=%wide.region_12.13_spmd, body=%wide.region_11.12_spmd.sunk | while | flops 176275456 | bytes 2367137 | solution.py:84
  465.5 1.5 convert_element_type.51
  (265 shorter events, 84.3 us)
Async XLA Ops:
  7.2 27.1 %copy-start = (bf16[256,1024]{1,0:T(8,128)(2,1)S(1)}, bf16[256,1024]{1,0:T(8,128)(2,1)}, u32[]{:S(2)}) copy-start(bf16[256,1024]{1,0:T(8,128)(2,1)} %param.20) | copy-start | bytes 1572868
  7.2 100.5 %all-gather.9.cloned.1.call-start = ((), (), s32[]{:S(2)}) async-start(), calls=%async_computation.3 | async-start | bytes 8519680 | tf_op jit(solution)/shard_map/all_gather | solution.py:15
  7.2 4.0 copy-start.8
  8.4 8.4 %copy-start.15 = (f32[2,2,64]{2,1,0:T(2,128)}, f32[2,2,64]{2,1,0:T(2,128)S(1)}, u32[]{:S(2)}) copy-start(f32[2,2,64]{2,1,0:T(2,128)S(1)} %fusion.97) | copy-start | bytes 3076
  9.4 7.4 %copy-start.14 = (f32[2,2,64]{2,1,0:T(2,128)}, f32[2,2,64]{2,1,0:T(2,128)S(1)}, u32[]{:S(2)}) copy-start(f32[2,2,64]{2,1,0:T(2,128)S(1)} %fusion.96) | copy-start | bytes 3076
  10.3 0.8 copy-start.10
  10.3 5.4 %copy-start.12 = (f32[2,2,64]{2,1,0:T(2,128)}, f32[2,2,64]{2,1,0:T(2,128)S(1)}, u32[]{:S(2)}) copy-start(f32[2,2,64]{2,1,0:T(2,128)S(1)} %get-tuple-element.713) | copy-start | bytes 3076
  11.6 0.6 copy-start.1
  15.0 0.6 copy-start.7
  21.5 168.7 %all-gather.11.cloned.1.call-start = ((), (), s32[]{:S(2)}) async-start(), calls=%async_computation.4 | async-start | bytes 8519680 | tf_op jit(solution)/shard_map/all_gather | solution.py:15
  22.3 250.7 %all-gather.13.cloned.1.call-start = ((), (), s32[]{:S(2)}) async-start(), calls=%async_computation.5 | async-start | bytes 8519680 | tf_op jit(solution)/shard_map/all_gather | solution.py:15
  23.1 332.2 %all-gather.15.cloned.1.call-start = ((), (), s32[]{:S(2)}) async-start(), calls=%async_computation.6 | async-start | bytes 8519680 | tf_op jit(solution)/shard_map/all_gather | solution.py:15
  36.5 429.0 %reduce-scatter.2.cloned.1.call-start = ((), (), s32[]{:S(2)}) async-start(), calls=%async_computation.2 | async-start | bytes 655360 | tf_op jit(solution)/shard_map/reduce_scatter | solution.py:164
  439.6 17.2 %copy-start.2 = (f32[2,2,64,64]{3,2,1,0:T(8,128)S(1)}, f32[2,2,64,64]{3,2,1,0:T(8,128)}, u32[]{:S(2)}) copy-start(f32[2,2,64,64]{3,2,1,0:T(8,128)} %copy-done.1) | copy-start | bytes 196612
  449.9 8.0 %copy-start.9 = (f32[64,64]{1,0:T(8,128)S(1)}, f32[64,64]{1,0:T(8,128)}, u32[]{:S(2)}) copy-start(f32[64,64]{1,0:T(8,128)} %copy-done.8) | copy-start | bytes 49156
  449.9 9.2 %copy-start.11 = (pred[64,64]{1,0:T(8,128)(4,1)S(1)}, pred[64,64]{1,0:T(8,128)(4,1)}, u32[]{:S(2)}) copy-start(pred[64,64]{1,0:T(8,128)(4,1)} %copy-done.10) | copy-start | bytes 12292
  449.9 10.0 %copy-start.5 = (f32[2,2,64,64]{3,2,1,0:T(8,128)S(1)}, f32[2,2,64,64]{3,2,1,0:T(8,128)}, u32[]{:S(2)}) copy-start(f32[2,2,64,64]{3,2,1,0:T(8,128)} %get-tuple-element.516) | copy-start | bytes 196612
  449.9 10.0 %copy-start.13 = (f32[2,2,64]{2,1,0:T(2,128)S(1)}, f32[2,2,64]{2,1,0:T(2,128)}, u32[]{:S(2)}) copy-start(f32[2,2,64]{2,1,0:T(2,128)} %copy-done.12) | copy-start | bytes 3076
  449.9 10.5 %copy-start.4 = (f32[2,2,64,128]{3,2,0,1:T(8,128)S(1)}, f32[2,2,64,128]{3,2,0,1:T(8,128)}, u32[]{:S(2)}) copy-start(f32[2,2,64,128]{3,2,0,1:T(8,128)} %get-tuple-element.517) | copy-start | bytes 393220
  449.9 11.0 %copy-start.16 = (f32[2,2,64]{2,1,0:T(2,128)S(1)}, f32[2,2,64]{2,1,0:T(2,128)}, u32[]{:S(2)}) copy-start(f32[2,2,64]{2,1,0:T(2,128)} %copy-done.15) | copy-start | bytes 3076
  449.9 12.5 %copy-start.6 = (f32[2,2,64,128]{3,2,1,0:T(8,128)S(1)}, f32[2,2,64,128]{3,2,1,0:T(8,128)}, u32[]{:S(2)}) copy-start(f32[2,2,64,128]{3,2,1,0:T(8,128)} %get-tuple-element.519) | copy-start | bytes 393220
  450.0 13.6 %copy-start.3 = (f32[2,2,64,128]{3,2,0,1:T(8,128)S(1)}, f32[2,2,64,128]{3,2,0,1:T(8,128)}, u32[]{:S(2)}) copy-start(f32[2,2,64,128]{3,2,0,1:T(8,128)} %get-tuple-element.515) | copy-start | bytes 393220
Sparse Core Ops, SparseCore 0:
  21.7 85.9 all-gather.8
  110.4 79.7 all-gather.10
  193.0 79.9 all-gather.12
  275.6 79.6 all-gather.14
  357.7 18.8 reduce-scatter.1
